TPU v7x, 256 devices: a whole 4x4x8 slice. The times are simulated.
256 devices in a mesh: gx: 32 (over z_hi, x, core), gy: 4 (over y), gz: 2 (over z_lo).
Axes of the slice: x: 4, y: 4, z: 8 (z_hi: 4, z_lo: 2; z = z_hi * 2 + z_lo), core: 2. Of those that a mesh axis runs over, the one named last changes fastest.
Arguments:
- unary: bfloat16 [128, 32, 128, 128], P('gx', 'gy', 'gz'), may hold values from -3 to 3
- compat: float32 [6, 128, 128], replicated, may hold values from -2.5 to 2.5
- saved_first: bfloat16 [6, 128, 32, 128, 128], P(None, 'gx', 'gy', 'gz'), may hold values from 0.25 to 4
- saved_second: bfloat16 [6, 128, 32, 128, 128], P(None, 'gx', 'gy', 'gz'), may hold values from 0.25 to 4
- cotangent: float32 [128, 32, 128, 128], P('gx', 'gy', 'gz'), may hold values from -6 to 6
Outputs:
- grad_unary: float32 [128, 32, 128, 128], P('gx', 'gy', 'gz')
- grad_compat: float32 [6, 128, 128], replicated
All inputs are finite; a program needn't handle non-finite values.
Results may differ from a plain program's by a relative error of at most 0.0084.
Values may be sent and summed in bfloat16 or wider, within the bound.
No kernel may reach another device: no remote copies, remote signals or barrier semaphores. Data moves between devices by JAX's collectives and lax.ppermute only.
A program may use at most 128 MiB of HBM per device.

v0:
```python
import jax
import jax.numpy as jnp
from jax import lax
from jax.sharding import PartitionSpec as P

OPPOSE = (1, 0, 3, 2, 5, 4)


def extended(cells, sides, width):
    for axis, dim in sides:
        count = lax.axis_size(axis)
        ends = count - 1
        head = lax.slice_in_dim(cells, 0, width, axis=dim)
        tail = lax.slice_in_dim(cells, cells.shape[dim] - width, cells.shape[dim], axis=dim)
        cells = jnp.concatenate(
            [
                lax.ppermute(tail, axis, [(i, (i + 1) % count) for i in range(ends)]),
                cells,
                lax.ppermute(head, axis, [((i + 1) % count, i) for i in range(ends)]),
            ],
            axis=dim,
        )
    return cells


def full_product(fields):
    result = fields[0]
    for index in range(1, 6):
        result = result * fields[index]
    return result


def send_terms(potential, messages, whole, weights_b):
    labels = potential.shape[-1]
    scaled = potential * whole
    hidden = [scaled / messages[OPPOSE[direction]] for direction in range(6)]
    hidden_b = jnp.stack(hidden).astype(jnp.bfloat16)
    outgoing = jnp.einsum(
        "dxyzk,dkl->dxyzl", hidden_b, weights_b, preferred_element_type=jnp.float32
    )
    totals = jnp.sum(outgoing, axis=-1, keepdims=True)
    normal = labels * outgoing / totals
    return (hidden_b, normal, totals)


def trade(low_face, high_face, axis_dim):
    packed = jnp.concatenate([low_face, high_face], axis=axis_dim)
    if axis_dim == 0:
        rims = extended(packed, (("gx", 0),), 1)
    elif axis_dim == 1:
        rims = extended(packed, (("gy", 1),), 1)
    else:
        rims = extended(packed, (("gz", 2),), 1)
    lower = lax.slice_in_dim(rims, 0, 1, axis=axis_dim)
    upper = lax.slice_in_dim(rims, 3, 4, axis=axis_dim)
    return (lower, upper)


def spread(normal_b, lower_edge, upper_edge):
    result = []
    for axis_dim in range(3):
        plus = normal_b[2 * axis_dim]
        minus = normal_b[2 * axis_dim + 1]
        length = plus.shape[axis_dim]
        lower, upper = trade(
            lax.slice_in_dim(minus, 0, 1, axis=axis_dim),
            lax.slice_in_dim(plus, length - 1, length, axis=axis_dim),
            axis_dim,
        )
        ones = jnp.ones_like(lower)
        lower = jnp.where(lower_edge[axis_dim], ones, lower)
        upper = jnp.where(upper_edge[axis_dim], ones, upper)
        result.append(
            jnp.concatenate(
                [lower, lax.slice_in_dim(plus, 0, length - 1, axis=axis_dim)], axis=axis_dim
            )
        )
        result.append(
            jnp.concatenate(
                [lax.slice_in_dim(minus, 1, length, axis=axis_dim), upper], axis=axis_dim
            )
        )
    return result


def gather_back(grad_b):
    result = []
    for axis_dim in range(3):
        plus = grad_b[2 * axis_dim]
        minus = grad_b[2 * axis_dim + 1]
        length = plus.shape[axis_dim]
        lower, upper = trade(
            lax.slice_in_dim(plus, 0, 1, axis=axis_dim),
            lax.slice_in_dim(minus, length - 1, length, axis=axis_dim),
            axis_dim,
        )
        result.append(
            jnp.concatenate(
                [lax.slice_in_dim(plus, 1, length, axis=axis_dim), upper], axis=axis_dim
            )
        )
        result.append(
            jnp.concatenate(
                [lower, lax.slice_in_dim(minus, 0, length - 1, axis=axis_dim)], axis=axis_dim
            )
        )
    return jnp.stack(result).astype(jnp.float32)


def belief_adjoint(potential, arriving, cotangent):
    labels = potential.shape[-1]
    whole = full_product(arriving)
    joint = potential * whole
    summed = jnp.sum(joint, axis=-1, keepdims=True)
    belief = joint / summed
    grad_joint = labels * (cotangent - jnp.sum(cotangent * belief, axis=-1, keepdims=True)) / summed
    grad_potential = grad_joint * whole
    scaled = grad_joint * joint
    grad_arriving = [(scaled / arriving[edge]).astype(jnp.bfloat16) for edge in range(6)]
    return (grad_arriving, grad_potential)


def local_adjoint(grad_normal, normal, totals, hidden_b, weights_b):
    labels = normal.shape[-1]
    inner = jnp.sum(grad_normal * normal, axis=-1, keepdims=True)
    grad_out = (labels / totals * (grad_normal - inner / labels)).astype(jnp.bfloat16)
    grad_weights = jnp.einsum(
        "dxyzk,dxyzl->dkl", hidden_b, grad_out, preferred_element_type=jnp.float32
    )
    grad_hidden = jnp.einsum(
        "dxyzl,dkl->dxyzk", grad_out, weights_b, preferred_element_type=jnp.float32
    )
    return (grad_weights, grad_hidden)


def adjoint_terms(grad_hidden, potential, messages, whole):
    ratios = [grad_hidden[OPPOSE[index]] / messages[index] for index in range(6)]
    total = ratios[0]
    for index in range(1, 6):
        total = total + ratios[index]
    unary_term = whole * total
    scaled = potential * whole
    grad_messages = []
    for edge in range(6):
        partial_sum = None
        for index in range(6):
            if index == edge:
                continue
            partial_sum = ratios[index] if partial_sum is None else partial_sum + ratios[index]
        grad_messages.append((partial_sum * (scaled / messages[edge])).astype(jnp.bfloat16))
    return (unary_term, grad_messages)


def body(unary, compat, saved_first, saved_second, cotangent):
    potential = jnp.exp(unary.astype(jnp.float32))
    weights = jnp.exp(compat)
    weights_b = weights.astype(jnp.bfloat16)
    lower_edge = (lax.axis_index("gx") == 0, lax.axis_index("gy") == 0, lax.axis_index("gz") == 0)
    upper_edge = (
        lax.axis_index("gx") == lax.axis_size("gx") - 1,
        lax.axis_index("gy") == lax.axis_size("gy") - 1,
        lax.axis_index("gz") == lax.axis_size("gz") - 1,
    )
    first = [saved_first[index].astype(jnp.float32) for index in range(6)]
    second = [saved_second[index].astype(jnp.float32) for index in range(6)]
    whole_two = full_product(second)
    hidden_two, normal_two, totals_two = send_terms(potential, second, whole_two, weights_b)
    arriving = spread(
        [normal_two[index].astype(jnp.bfloat16) for index in range(6)], lower_edge, upper_edge
    )
    arriving = [value.astype(jnp.float32) for value in arriving]
    grad_arriving, grad_potential = belief_adjoint(potential, arriving, cotangent)
    grad_normal_two = gather_back(grad_arriving)
    weights_two, grad_hidden_two = local_adjoint(
        grad_normal_two, normal_two, totals_two, hidden_two, weights_b
    )
    unary_two, grad_second = adjoint_terms(grad_hidden_two, potential, second, whole_two)
    grad_potential = grad_potential + unary_two
    whole_one = full_product(first)
    hidden_one, normal_one, totals_one = send_terms(potential, first, whole_one, weights_b)
    grad_normal_one = gather_back(grad_second)
    weights_one, grad_hidden_one = local_adjoint(
        grad_normal_one, normal_one, totals_one, hidden_one, weights_b
    )
    ratios_one = [grad_hidden_one[OPPOSE[index]] / first[index] for index in range(6)]
    total_one = ratios_one[0]
    for index in range(1, 6):
        total_one = total_one + ratios_one[index]
    grad_potential = grad_potential + whole_one * total_one
    grad_unary = potential * grad_potential
    summed = lax.psum(weights_two + weights_one, ("gx", "gy", "gz"))
    grad_compat = weights * summed
    return (grad_unary, grad_compat)


def solution(mesh):
    placed = (
        P("gx", "gy", "gz", None),
        P(),
        P(None, "gx", "gy", "gz", None),
        P(None, "gx", "gy", "gz", None),
        P("gx", "gy", "gz", None),
    )
    return jax.shard_map(
        body,
        mesh=mesh,
        in_specs=placed,
        out_specs=(P("gx", "gy", "gz", None), P()),
        check_vma=False,
    )
```

profile of v0, /device:TPU:1, one launch (start us, length us, event | category | flops | bytes accessed | tf_op | source)
XLA Modules:
  0.0 413.3 jit_solution(10263491536333653765)
XLA Ops:
  7.2 4.7 %bitcast_dynamic-update-slice_fusion.5 = (bf16[6,4,8,64,128]{4,3,2,1,0:T(8,128)(2,1)S(1)}, f32[4,8,64,128]{3,2,1,0:T(8,128)S(1)}, bf16[6,4,8,64,128]{4,3,2,1,0:T(8,128)(2,1)S(1)}, f32[4,8,64,128]{3,2,1,0:T(8,128)S(1)}) fusion(bf16[6,4,8,64,128]{4,3,2,1,0:T(8,128)(2,1)} %param.7, bf16[4,8,64,128]{3,2,1,0:T(8,128)(2,1)} %param.5, ...), kind=kLoop, calls=%fused_computation.152 | loop fusion | flops 7602174 | bytes 9961472
  11.9 0.2 bitcast_dynamic-update-slice_fusion.10
  12.2 0.2 bitcast_dynamic-update-slice_fusion.9
  12.4 0.2 bitcast_dynamic-update-slice_fusion.8
  12.6 0.2 bitcast_dynamic-update-slice_fusion.7
  12.9 1.2 copy-done.3
  14.1 0.2 bitcast_dynamic-update-slice_fusion.4
  14.3 0.2 bitcast_dynamic-update-slice_fusion.3
  14.6 0.4 bitcast_dynamic-update-slice_fusion.2
  15.0 1.9 fusion.77
  17.0 2.0 fusion.13
  19.0 0.6 copy-done.2
  19.8 0.7 slice.293
  20.5 1.3 collective-permute-start.3
  21.7 0.6 slice.289
  22.4 5.3 %collective-permute-start.2 = (bf16[4,1,64,128]{3,2,1,0:T(8,128)(2,1)}, bf16[4,1,64,128]{3,2,1,0:T(8,128)(2,1)}, u32[]{:S(2)}, u32[]{:S(2)}) collective-permute-start(bf16[4,1,64,128]{3,2,1,0:T(8,128)(2,1)} %slice.289), channel_id=1, source_target_pairs={{0,2},{2,4},{4,6},{1,3},{3,5},{5,7},{8,10},{10,12},{12,14},{9,11},... | collective-permute-start | bytes 196616 | tf_op jit(solution)/shard_map/ppermute | solution.py:17
  27.6 0.6 slice.299
  28.2 1.3 collective-permute-start.5
  29.5 0.6 slice.295
  30.1 4.6 %collective-permute-start.4 = (bf16[4,8,1,128]{3,2,1,0:T(2,128)(2,1)}, bf16[4,8,1,128]{3,2,1,0:T(2,128)(2,1)S(1)}, u32[]{:S(2)}, u32[]{:S(2)}) collective-permute-start(bf16[4,8,1,128]{3,2,1,0:T(2,128)(2,1)} %slice.295), channel_id=1, source_target_pairs={{0,1},{2,3},{4,5},{6,7},{8,9},{10,11},{12,13},{14,15},{16,17},{18,... | collective-permute-start | bytes 24584 | tf_op jit(solution)/shard_map/ppermute | solution.py:17
  34.7 0.7 slice_bitcast_fusion.19
  35.4 5.6 %collective-permute-start.1 = (bf16[1,8,64,128]{3,2,1,0:T(8,128)(2,1)}, bf16[1,8,64,128]{3,2,1,0:T(8,128)(2,1)}, u32[]{:S(2)}, u32[]{:S(2)}) collective-permute-start(bf16[1,8,64,128]{3,2,1,0:T(8,128)(2,1)} %get-tuple-element.20), channel_id=1, source_target_pairs={{8,0},{16,8},{24,16},{32,24},{40,32},{48,40},{56,48},{64,56},{72,6... | collective-permute-start | bytes 393224 | tf_op jit(solution)/shard_map/ppermute | solution.py:19
  41.0 0.9 slice_bitcast_fusion.17
  41.9 0.2 bitcast_dynamic-update-slice_fusion.1
  42.1 0.2 bitcast_dynamic-update-slice_fusion
  42.4 4.4 %fusion.78 = (f32[6,4,8,64]{3,2,1,0:T(8,128)S(1)}, f32[6,4,8,64,128]{4,3,2,1,0:T(8,128)}) fusion(bf16[6,4,8,64,128]{4,3,2,1,0:T(8,128)(2,1)S(1)} %bitcast_dynamic-update-slice_fusion, bf16[6,128,128,1,1]{2,1,4,3,0:T(8,128)(2,1)S(1)} %fusion.68), kind=kOutput, calls=%fused_computation.182 | convolution fusion | flops 404213760 | bytes 9682944 | tf_op jit(solution)/shard_map/dxyzk,dkl->dxyzl/dot_general | solution.py:38
  46.8 0.6 broadcast_divide_fusion.1
  47.4 1.0 slice.298
  48.4 1.1 slice.292
  49.5 2.2 collective-permute-start
  51.8 0.8 broadcast_select_fusion.4
  52.6 0.9 broadcast_select_fusion.2
  53.5 0.9 broadcast_select_fusion
  54.4 2.0 fusion.72
  56.5 11.9 %fusion.37 = (bf16[4,8,64,128]{3,2,1,0:T(8,128)(2,1)S(1)}, f32[4,8,64,128]{3,2,1,0:T(8,128)S(1)}, f32[4,8,64,128]{3,2,1,0:T(8,128)}) fusion(bf16[4,8,1,128]{3,2,1,0:T(2,128)(2,1)S(1)} %broadcast_select_fusion.4, bf16[4,8,63,128]{3,2,1,0:T(8,128)(2,1)S(1)} %copy-done.14, f32[4,8,64,128]{3,2,1,0:T(8,128)S(1)} %get-tuple-element.13, ...), kind=kOutput, calls=%fused_computation.75 | output fusion | flops 4196479 | bytes 5775360 | tf_op jit(solution)/shard_map/sub | solution.py:116
  68.4 0.8 fusion.36
  69.3 2.5 collective-permute-start.6
  71.8 3.2 collective-permute-start.7
  75.4 1.4 collective-permute-start.8
  76.8 4.0 collective-permute-start.9
  80.8 1.3 collective-permute-start.10
  82.2 4.0 collective-permute-start.11
  86.6 0.4 collective-permute-done.11
  87.0 0.2 fusion.60
  87.3 3.8 fusion.1
  91.1 5.5 %fusion.79 = f32[6,4,8,64,128]{4,3,2,1,0:T(8,128)S(1)} fusion(bf16[6,128,128,1,1]{2,1,4,3,0:T(8,128)(2,1)S(1)} %fusion.68, bf16[6,4,8,64,128]{4,3,2,1,0:T(8,128)(2,1)S(1)} %fusion.60, f32[6,4,8,64]{3,2,1,0:T(8,128)S(1)} %broadcast_multiply_fusion.1, f32[6,4,8,64]{3,2,1,0:T(8,128)S(1)} %copy-done.18), kind=kOutput, calls=%fused_computation.183 | convolution fusion | flops 408944640 | bytes 9732096 | tf_op jit(solution)/shard_map/dxyzl,dkl->dxyzk/dot_general | solution.py:130
  96.6 1.1 multiply_convert_fusion
  97.7 0.5 multiply_convert_fusion.1
  98.2 1.0 multiply_convert_fusion.5
  99.2 1.2 multiply_convert_fusion.2
  100.4 4.2 %collective-permute-start.13 = (bf16[1,8,64,128]{3,2,1,0:T(8,128)(2,1)S(1)}, bf16[1,8,64,128]{3,2,1,0:T(8,128)(2,1)S(1)}, u32[]{:S(2)}, u32[]{:S(2)}) collective-permute-start(bf16[1,8,64,128]{3,2,1,0:T(8,128)(2,1)S(1)} %slice.320), channel_id=1, source_target_pairs={{0,8},{8,16},{16,24},{24,32},{32,40},{40,48},{48,56},{56,64},{64,7... | collective-permute-start | bytes 393224 | tf_op jit(solution)/shard_map/ppermute | solution.py:17
  104.7 2.2 collective-permute-start.12
  106.9 5.7 %fusion.17 = f32[6,128,128]{2,1,0:T(8,128)S(1)} fusion(bf16[6,4,8,64,128]{4,3,2,1,0:T(8,128)(2,1)S(1)} %copy-done.10, bf16[6,4,8,64,128]{4,3,2,1,0:T(8,128)(2,1)S(1)} %fusion.60, f32[6,4,8,64]{3,2,1,0:T(8,128)S(1)} %broadcast_multiply_fusion.1, f32[6,4,8,64]{3,2,1,0:T(8,128)S(1)} %copy-done.18), kind=kOutput, calls=%fused_computation.67 | convolution fusion | flops 408944640 | bytes 6782976 | tf_op jit(solution)/shard_map/dxyzk,dxyzl->dkl/dot_general | solution.py:127
  112.9 1.3 collective-permute-start.14
  114.2 4.0 collective-permute-start.15
  118.2 1.3 collective-permute-start.16
  119.5 4.2 %collective-permute-start.17 = (bf16[4,8,1,128]{3,2,1,0:T(2,128)(2,1)S(1)}, bf16[4,8,1,128]{3,2,1,0:T(2,128)(2,1)S(1)}, u32[]{:S(2)}, u32[]{:S(2)}) collective-permute-start(bf16[4,8,1,128]{3,2,1,0:T(2,128)(2,1)S(1)} %slice.328), channel_id=1, source_target_pairs={{0,1},{2,3},{4,5},{6,7},{8,9},{10,11},{12,13},{14,15},{16,17},{18,... | collective-permute-start | bytes 24584 | tf_op jit(solution)/shard_map/ppermute | solution.py:17
  124.4 0.2 fusion.66
  124.6 3.8 fusion.4
  128.5 6.8 %fusion.80 = f32[6,4,8,64,128]{4,3,2,1,0:T(8,128)} fusion(bf16[6,128,128,1,1]{2,1,4,3,0:T(8,128)(2,1)S(1)} %fusion.68, bf16[6,4,8,64,128]{4,3,2,1,0:T(8,128)(2,1)S(1)} %fusion.66, f32[6,4,8,64]{3,2,1,0:T(8,128)S(1)} %broadcast_multiply_fusion, f32[6,4,8,64]{3,2,1,0:T(8,128)S(1)} %broadcast_divide_fusion), kind=kOutput, calls=%fused_computation.184 | convolution fusion | flops 408944640 | bytes 9732096 | tf_op jit(solution)/shard_map/dxyzl,dkl->dxyzk/dot_general | solution.py:130
  135.3 6.2 %fusion.27 = f32[6,128,128]{2,1,0:T(8,128)} fusion(f32[6,128,128]{2,1,0:T(8,128)S(1)} %fusion.17, bf16[6,4,8,64,128]{4,3,2,1,0:T(8,128)(2,1)S(1)} %copy-done.8, bf16[6,4,8,64,128]{4,3,2,1,0:T(8,128)(2,1)S(1)} %fusion.66, f32[6,4,8,64]{3,2,1,0:T(8,128)S(1)} %broadcast_multiply_fusion, f32[6,4,8,64]{3,2,1,0:T(8,128)S(1)} %broadcast_divide_fusion), kind=kOutput, calls=%fused_computation.69 | convolution fusion | flops 409042944 | bytes 7176192 | tf_op jit(solution)/shard_map/dxyzk,dxyzl->dkl/dot_general | solution.py:127
  141.5 7.3 %fusion.46 = f32[4,8,64,128]{3,2,1,0:T(8,128)} fusion(f32[6,4,8,64,128]{4,3,2,1,0:T(8,128)} %fusion.80, f32[4,8,64,128]{3,2,1,0:T(8,128)S(1)} %get-tuple-element.9, f32[4,8,64,128]{3,2,1,0:T(8,128)} %get-tuple-element.36, f32[4,8,64,128]{3,2,1,0:T(8,128)} %copy-done.11, bf16[4,8,64,128]{3,2,1,0:T(8,128)(2,1)} %param.5, f32[4,8,64,128]{3,2,1,0:T(8,128)S(1)} %copy-done.5, ...), kind=kLoop, calls=%fused_computation.84 | loop fusion | flops 11010048 | bytes 19398656 | tf_op jit(solution)/shard_map/mul | solution.py:190
  148.9 255.7 %all-reduce.2.cloned.1.call-done = f32[6,128,128]{2,1,0:T(8,128)} async-done(((f32[6,128,128]{2,1,0:T(8,128)}), f32[6,128,128]{2,1,0:T(8,128)}) %all-reduce.2.cloned.1.call-update) | async-done | bytes 393232 | tf_op jit(solution)/shard_map/psum | solution.py:191
  404.5 1.9 exponential_multiply_fusion
  (109 shorter events, 2.2 us)
Async XLA Ops:
  7.2 397.4 %all-reduce.2.cloned.1.call-start = ((), (), s32[]{:S(2)}) async-start(), calls=%async_computation | async-start | bytes 786432 | tf_op jit(solution)/shard_map/psum | solution.py:191
  7.2 4.7 %copy-start = (bf16[6,4,8,64,128]{4,3,2,1,0:T(8,128)(2,1)S(1)}, bf16[6,4,8,64,128]{4,3,2,1,0:T(8,128)(2,1)}, u32[]{:S(2)}) copy-start(bf16[6,4,8,64,128]{4,3,2,1,0:T(8,128)(2,1)} %param.8) | copy-start | bytes 9437188
  12.2 1.9 copy-start.3
  12.6 1.9 copy-start.17
  15.0 1.9 copy-start.9
  16.9 2.7 copy-start.2
  19.8 22.6 %copy-start.16 = (bf16[4,8,64,128]{3,2,1,0:T(8,128)(2,1)}, bf16[4,8,64,128]{3,2,1,0:T(8,128)(2,1)S(1)}, u32[]{:S(2)}) copy-start(bf16[4,8,64,128]{3,2,1,0:T(8,128)(2,1)S(1)} %get-tuple-element.26) | copy-start | bytes 1572868
  20.5 32.1 %collective-permute-start.3 = (bf16[4,1,64,128]{3,2,1,0:T(8,128)(2,1)}, bf16[4,1,64,128]{3,2,1,0:T(8,128)(2,1)}, u32[]{:S(2)}, u32[]{:S(2)}) collective-permute-start(bf16[4,1,64,128]{3,2,1,0:T(8,128)(2,1)} %slice.293), channel_id=1, source_target_pairs={{2,0},{4,2},{6,4},{3,1},{5,3},{7,5},{10,8},{12,10},{14,12},{11,9},... | collective-permute-start | bytes 196616 | tf_op jit(solution)/shard_map/ppermute | solution.py:19
  22.4 31.1 %collective-permute-start.2 = (bf16[4,1,64,128]{3,2,1,0:T(8,128)(2,1)}, bf16[4,1,64,128]{3,2,1,0:T(8,128)(2,1)}, u32[]{:S(2)}, u32[]{:S(2)}) collective-permute-start(bf16[4,1,64,128]{3,2,1,0:T(8,128)(2,1)} %slice.289), channel_id=1, source_target_pairs={{0,2},{2,4},{4,6},{1,3},{3,5},{5,7},{8,10},{10,12},{12,14},{9,11},... | collective-permute-start | bytes 196616 | tf_op jit(solution)/shard_map/ppermute | solution.py:17
  28.2 21.3 %collective-permute-start.5 = (bf16[4,8,1,128]{3,2,1,0:T(2,128)(2,1)}, bf16[4,8,1,128]{3,2,1,0:T(2,128)(2,1)}, u32[]{:S(2)}, u32[]{:S(2)}) collective-permute-start(bf16[4,8,1,128]{3,2,1,0:T(2,128)(2,1)} %slice.299), channel_id=1, source_target_pairs={{1,0},{3,2},{5,4},{7,6},{9,8},{11,10},{13,12},{15,14},{17,16},{19,... | collective-permute-start | bytes 24584 | tf_op jit(solution)/shard_map/ppermute | solution.py:19
  30.1 22.4 %collective-permute-start.4 = (bf16[4,8,1,128]{3,2,1,0:T(2,128)(2,1)}, bf16[4,8,1,128]{3,2,1,0:T(2,128)(2,1)S(1)}, u32[]{:S(2)}, u32[]{:S(2)}) collective-permute-start(bf16[4,8,1,128]{3,2,1,0:T(2,128)(2,1)} %slice.295), channel_id=1, source_target_pairs={{0,1},{2,3},{4,5},{6,7},{8,9},{10,11},{12,13},{14,15},{16,17},{18,... | collective-permute-start | bytes 24584 | tf_op jit(solution)/shard_map/ppermute | solution.py:17
  35.4 18.0 %collective-permute-start.1 = (bf16[1,8,64,128]{3,2,1,0:T(8,128)(2,1)}, bf16[1,8,64,128]{3,2,1,0:T(8,128)(2,1)}, u32[]{:S(2)}, u32[]{:S(2)}) collective-permute-start(bf16[1,8,64,128]{3,2,1,0:T(8,128)(2,1)} %get-tuple-element.20), channel_id=1, source_target_pairs={{8,0},{16,8},{24,16},{32,24},{40,32},{48,40},{56,48},{64,56},{72,6... | collective-permute-start | bytes 393224 | tf_op jit(solution)/shard_map/ppermute | solution.py:19
  42.4 4.4 %copy-start.7 = (bf16[6,4,8,64,128]{4,3,2,1,0:T(8,128)(2,1)}, bf16[6,4,8,64,128]{4,3,2,1,0:T(8,128)(2,1)S(1)}, u32[]{:S(2)}) copy-start(bf16[6,4,8,64,128]{4,3,2,1,0:T(8,128)(2,1)S(1)} %bitcast_dynamic-update-slice_fusion) | copy-start | bytes 9437188
  46.8 7.7 %copy-start.6 = (bf16[4,8,64,128]{3,2,1,0:T(8,128)(2,1)S(1)}, bf16[4,8,64,128]{3,2,1,0:T(8,128)(2,1)}, u32[]{:S(2)}) copy-start(bf16[4,8,64,128]{3,2,1,0:T(8,128)(2,1)} %param.5) | copy-start | bytes 1572868
  49.5 7.0 %copy-start.14 = (bf16[4,8,63,128]{3,2,1,0:T(8,128)(2,1)S(1)}, bf16[4,8,63,128]{3,2,1,0:T(8,128)(2,1)}, u32[]{:S(2)}) copy-start(bf16[4,8,63,128]{3,2,1,0:T(8,128)(2,1)} %slice.298) | copy-start | bytes 1548292
  49.5 7.0 %copy-start.19 = (f32[4,8,64,128]{3,2,1,0:T(8,128)S(1)}, f32[4,8,64,128]{3,2,1,0:T(8,128)}, u32[]{:S(2)}) copy-start(f32[4,8,64,128]{3,2,1,0:T(8,128)} %param.9) | copy-start | bytes 3145732
  49.5 4.9 %collective-permute-start = (bf16[1,8,64,128]{3,2,1,0:T(8,128)(2,1)}, bf16[1,8,64,128]{3,2,1,0:T(8,128)(2,1)S(1)}, u32[]{:S(2)}, u32[]{:S(2)}) collective-permute-start(bf16[1,8,64,128]{3,2,1,0:T(8,128)(2,1)} %get-tuple-element.19), channel_id=1, source_target_pairs={{0,8},{8,16},{16,24},{24,32},{32,40},{40,48},{48,56},{56,64},{64,7... | collective-permute-start | bytes 393224 | tf_op jit(solution)/shard_map/ppermute | solution.py:17
  56.5 11.9 %copy-start.11 = (f32[4,8,64,128]{3,2,1,0:T(8,128)}, f32[4,8,64,128]{3,2,1,0:T(8,128)S(1)}, u32[]{:S(2)}) copy-start(f32[4,8,64,128]{3,2,1,0:T(8,128)S(1)} %get-tuple-element.13) | copy-start | bytes 3145732
  56.5 11.9 %copy-start.12 = (bf16[3,8,64,128]{3,2,1,0:T(8,128)(2,1)S(1)}, bf16[3,8,64,128]{3,2,1,0:T(8,128)(2,1)}, u32[]{:S(2)}) copy-start(bf16[3,8,64,128]{3,2,1,0:T(8,128)(2,1)} %get-tuple-element.21) | copy-start | bytes 1179652
  56.5 11.9 %copy-start.13 = (bf16[3,8,64,128]{3,2,1,0:T(8,128)(2,1)S(1)}, bf16[3,8,64,128]{3,2,1,0:T(8,128)(2,1)}, u32[]{:S(2)}) copy-start(bf16[3,8,64,128]{3,2,1,0:T(8,128)(2,1)} %get-tuple-element.22) | copy-start | bytes 1179652
  68.4 18.9 %slice-start = ((s8[6291456]{0:T(1024)(128)(4,1)}), s8[4194304]{0:T(1024)(128)(4,1)S(1)}, s32[]{:S(2)}) async-start(s8[6291456]{0:T(1024)(128)(4,1)} %bitcast.353), calls=%async_computation.1 | async-start | bytes 8388608
  69.3 12.9 %collective-permute-start.6 = (bf16[1,8,64,128]{3,2,1,0:T(8,128)(2,1)S(1)}, bf16[1,8,64,128]{3,2,1,0:T(8,128)(2,1)S(1)}, u32[]{:S(2)}, u32[]{:S(2)}) collective-permute-start(bf16[1,8,64,128]{3,2,1,0:T(8,128)(2,1)S(1)} %slice.301), channel_id=1, source_target_pairs={{8,0},{16,8},{24,16},{32,24},{40,32},{48,40},{56,48},{64,56},{72,6... | collective-permute-start | bytes 393224 | tf_op jit(solution)/shard_map/ppermute | solution.py:19
  71.8 14.4 %collective-permute-start.7 = (bf16[1,8,64,128]{3,2,1,0:T(8,128)(2,1)S(1)}, bf16[1,8,64,128]{3,2,1,0:T(8,128)(2,1)S(1)}, u32[]{:S(2)}, u32[]{:S(2)}) collective-permute-start(bf16[1,8,64,128]{3,2,1,0:T(8,128)(2,1)S(1)} %slice.302), channel_id=1, source_target_pairs={{0,8},{8,16},{16,24},{24,32},{32,40},{40,48},{48,56},{56,64},{64,7... | collective-permute-start | bytes 393224 | tf_op jit(solution)/shard_map/ppermute | solution.py:17
  75.1 12.2 %slice-start.1 = ((s8[6291456]{0:T(1024)(128)(4,1)}), s8[2097152]{0:T(1024)(128)(4,1)S(1)}, s32[]{:S(2)}) async-start(s8[6291456]{0:T(1024)(128)(4,1)} %bitcast.353), calls=%async_computation.2 | async-start | bytes 4194304
  75.4 10.9 %collective-permute-start.8 = (bf16[4,1,64,128]{3,2,1,0:T(8,128)(2,1)S(1)}, bf16[4,1,64,128]{3,2,1,0:T(8,128)(2,1)S(1)}, u32[]{:S(2)}, u32[]{:S(2)}) collective-permute-start(bf16[4,1,64,128]{3,2,1,0:T(8,128)(2,1)S(1)} %slice.305), channel_id=1, source_target_pairs={{2,0},{4,2},{6,4},{3,1},{5,3},{7,5},{10,8},{12,10},{14,12},{11,9},... | collective-permute-start | bytes 196616 | tf_op jit(solution)/shard_map/ppermute | solution.py:19
  76.8 9.6 %collective-permute-start.9 = (bf16[4,1,64,128]{3,2,1,0:T(8,128)(2,1)S(1)}, bf16[4,1,64,128]{3,2,1,0:T(8,128)(2,1)S(1)}, u32[]{:S(2)}, u32[]{:S(2)}) collective-permute-start(bf16[4,1,64,128]{3,2,1,0:T(8,128)(2,1)S(1)} %slice.306), channel_id=1, source_target_pairs={{0,2},{2,4},{4,6},{1,3},{3,5},{5,7},{8,10},{10,12},{12,14},{9,11},... | collective-permute-start | bytes 196616 | tf_op jit(solution)/shard_map/ppermute | solution.py:17
  80.8 5.6 %collective-permute-start.10 = (bf16[4,8,1,128]{3,2,1,0:T(2,128)(2,1)S(1)}, bf16[4,8,1,128]{3,2,1,0:T(2,128)(2,1)S(1)}, u32[]{:S(2)}, u32[]{:S(2)}) collective-permute-start(bf16[4,8,1,128]{3,2,1,0:T(2,128)(2,1)S(1)} %slice.309), channel_id=1, source_target_pairs={{1,0},{3,2},{5,4},{7,6},{9,8},{11,10},{13,12},{15,14},{17,16},{19,... | collective-permute-start | bytes 24584 | tf_op jit(solution)/shard_map/ppermute | solution.py:19
  82.2 4.8 %collective-permute-start.11 = (bf16[4,8,1,128]{3,2,1,0:T(2,128)(2,1)S(1)}, bf16[4,8,1,128]{3,2,1,0:T(2,128)(2,1)S(1)}, u32[]{:S(2)}, u32[]{:S(2)}) collective-permute-start(bf16[4,8,1,128]{3,2,1,0:T(2,128)(2,1)S(1)} %slice.310), channel_id=1, source_target_pairs={{0,1},{2,3},{4,5},{6,7},{8,9},{10,11},{12,13},{14,15},{16,17},{18,... | collective-permute-start | bytes 24584 | tf_op jit(solution)/shard_map/ppermute | solution.py:17
  87.3 3.8 copy-start.18
  91.1 5.5 %copy-start.1 = (bf16[6,4,8,64,128]{4,3,2,1,0:T(8,128)(2,1)S(1)}, bf16[6,4,8,64,128]{4,3,2,1,0:T(8,128)(2,1)}, u32[]{:S(2)}) copy-start(bf16[6,4,8,64,128]{4,3,2,1,0:T(8,128)(2,1)} %param.8) | copy-start | bytes 9437188
  97.7 1.4 copy-start.4
  99.2 13.4 %copy-start.15 = (bf16[4,8,64,128]{3,2,1,0:T(8,128)(2,1)}, bf16[4,8,64,128]{3,2,1,0:T(8,128)(2,1)S(1)}, u32[]{:S(2)}) copy-start(bf16[4,8,64,128]{3,2,1,0:T(8,128)(2,1)S(1)} %multiply_convert_fusion.5) | copy-start | bytes 1572868
  99.2 7.7 %copy-start.10 = (bf16[6,4,8,64,128]{4,3,2,1,0:T(8,128)(2,1)S(1)}, bf16[6,4,8,64,128]{4,3,2,1,0:T(8,128)(2,1)}, u32[]{:S(2)}) copy-start(bf16[6,4,8,64,128]{4,3,2,1,0:T(8,128)(2,1)} %copy-done.9) | copy-start | bytes 9437188
  99.2 25.4 %slice-start.2 = ((s8[6291456]{0:T(1024)(128)(4,1)}), s8[2097152]{0:T(1024)(128)(4,1)S(1)}, s32[]{:S(2)}) async-start(s8[6291456]{0:T(1024)(128)(4,1)} %bitcast.355), calls=%async_computation.3 | async-start | bytes 4194304
  100.4 23.4 %collective-permute-start.13 = (bf16[1,8,64,128]{3,2,1,0:T(8,128)(2,1)S(1)}, bf16[1,8,64,128]{3,2,1,0:T(8,128)(2,1)S(1)}, u32[]{:S(2)}, u32[]{:S(2)}) collective-permute-start(bf16[1,8,64,128]{3,2,1,0:T(8,128)(2,1)S(1)} %slice.320), channel_id=1, source_target_pairs={{0,8},{8,16},{16,24},{24,32},{32,40},{40,48},{48,56},{56,64},{64,7... | collective-permute-start | bytes 393224 | tf_op jit(solution)/shard_map/ppermute | solution.py:17
  104.7 20.0 %slice-start.3 = ((s8[6291456]{0:T(1024)(128)(4,1)}), s8[4194304]{0:T(1024)(128)(4,1)S(1)}, s32[]{:S(2)}) async-start(s8[6291456]{0:T(1024)(128)(4,1)} %bitcast.355), calls=%async_computation.4 | async-start | bytes 8388608
  104.7 14.9 %collective-permute-start.12 = (bf16[1,8,64,128]{3,2,1,0:T(8,128)(2,1)S(1)}, bf16[1,8,64,128]{3,2,1,0:T(8,128)(2,1)S(1)}, u32[]{:S(2)}, u32[]{:S(2)}) collective-permute-start(bf16[1,8,64,128]{3,2,1,0:T(8,128)(2,1)S(1)} %slice.319), channel_id=1, source_target_pairs={{8,0},{16,8},{24,16},{32,24},{40,32},{48,40},{56,48},{64,56},{72,6... | collective-permute-start | bytes 393224 | tf_op jit(solution)/shard_map/ppermute | solution.py:19
  112.6 11.2 %slice-start.4 = ((bf16[4,8,64,128]{3,2,1,0:T(8,128)(2,1)}), bf16[3,8,64,128]{3,2,1,0:T(8,128)(2,1)S(1)}, s32[]{:S(2)}) async-start(bf16[4,8,64,128]{3,2,1,0:T(8,128)(2,1)} %copy-done.15), calls=%async_computation.5 | async-start | bytes 786432 | tf_op jit(solution)/shard_map/slice | solution.py:99
  112.9 11.0 %collective-permute-start.14 = (bf16[4,1,64,128]{3,2,1,0:T(8,128)(2,1)S(1)}, bf16[4,1,64,128]{3,2,1,0:T(8,128)(2,1)S(1)}, u32[]{:S(2)}, u32[]{:S(2)}) collective-permute-start(bf16[4,1,64,128]{3,2,1,0:T(8,128)(2,1)S(1)} %slice.323), channel_id=1, source_target_pairs={{2,0},{4,2},{6,4},{3,1},{5,3},{7,5},{10,8},{12,10},{14,12},{11,9},... | collective-permute-start | bytes 196616 | tf_op jit(solution)/shard_map/ppermute | solution.py:19
  114.2 9.8 %collective-permute-start.15 = (bf16[4,1,64,128]{3,2,1,0:T(8,128)(2,1)S(1)}, bf16[4,1,64,128]{3,2,1,0:T(8,128)(2,1)S(1)}, u32[]{:S(2)}, u32[]{:S(2)}) collective-permute-start(bf16[4,1,64,128]{3,2,1,0:T(8,128)(2,1)S(1)} %slice.324), channel_id=1, source_target_pairs={{0,2},{2,4},{4,6},{1,3},{3,5},{5,7},{8,10},{10,12},{12,14},{9,11},... | collective-permute-start | bytes 196616 | tf_op jit(solution)/shard_map/ppermute | solution.py:17
  118.2 5.9 %collective-permute-start.16 = (bf16[4,8,1,128]{3,2,1,0:T(2,128)(2,1)S(1)}, bf16[4,8,1,128]{3,2,1,0:T(2,128)(2,1)S(1)}, u32[]{:S(2)}, u32[]{:S(2)}) collective-permute-start(bf16[4,8,1,128]{3,2,1,0:T(2,128)(2,1)S(1)} %slice.327), channel_id=1, source_target_pairs={{1,0},{3,2},{5,4},{7,6},{9,8},{11,10},{13,12},{15,14},{17,16},{19,... | collective-permute-start | bytes 24584 | tf_op jit(solution)/shard_map/ppermute | solution.py:19
  119.5 4.8 %collective-permute-start.17 = (bf16[4,8,1,128]{3,2,1,0:T(2,128)(2,1)S(1)}, bf16[4,8,1,128]{3,2,1,0:T(2,128)(2,1)S(1)}, u32[]{:S(2)}, u32[]{:S(2)}) collective-permute-start(bf16[4,8,1,128]{3,2,1,0:T(2,128)(2,1)S(1)} %slice.328), channel_id=1, source_target_pairs={{0,1},{2,3},{4,5},{6,7},{8,9},{10,11},{12,13},{14,15},{16,17},{18,... | collective-permute-start | bytes 24584 | tf_op jit(solution)/shard_map/ppermute | solution.py:17
  128.5 6.8 %copy-start.8 = (bf16[6,4,8,64,128]{4,3,2,1,0:T(8,128)(2,1)S(1)}, bf16[6,4,8,64,128]{4,3,2,1,0:T(8,128)(2,1)}, u32[]{:S(2)}) copy-start(bf16[6,4,8,64,128]{4,3,2,1,0:T(8,128)(2,1)} %copy-done.7) | copy-start | bytes 9437188
  135.3 6.3 %copy-start.5 = (f32[4,8,64,128]{3,2,1,0:T(8,128)S(1)}, f32[4,8,64,128]{3,2,1,0:T(8,128)}, u32[]{:S(2)}) copy-start(f32[4,8,64,128]{3,2,1,0:T(8,128)} %copy-done.4) | copy-start | bytes 3145732
Sparse Core Ops, SparseCore 0:
  141.7 262.8 all-reduce.1
where the time goes:
time: 414 us; the launch traced here: 413 us
  waiting for transfers between devices  256 us (62%)
  starting transfers between devices  53.8 us (13%)
  other arithmetic  48.6 us (12%)
  matrix products  30.4 us (7%)
  between operations  15.1 us (4%)
  local copies, waits for them, and re-layouts  9.02 us (2%)
    psum x1, waiting for transfers between devices, body(): summed = lax.psum(weights_two + weights_one, ('gx', 'gy', 'gz'))  256 us
    ppermute x9, starting transfers between devices, extended(): lax.ppermute(tail, axis, [(i, (i + 1) % count) for i in range(ends)])  35.6 us
    ppermute x9, starting transfers between devices, extended(): lax.ppermute(head, axis, [((i + 1) % count, i) for i in range(ends)])  18.1 us
    dot_general x2, matrix products, local_adjoint(): jnp.einsum('dxyzl,dkl->dxyzk', grad_out, weights_b, preferred_element_typ...  12.3 us
    dot_general x2, matrix products, local_adjoint(): jnp.einsum('dxyzk,dxyzl->dkl', hidden_b, grad_out, preferred_element_type...  11.9 us
    sub x1, other arithmetic, belief_adjoint(): cotangent - jnp.sum(cotangent * belief, axis=-1, keepdims=True)  11.9 us
  transfers between devices with their start and end apart: 19, of which 3 were waited for; matrix products, arithmetic and copies ran while one was open for 7% of the time, Pallas kernels for 0%

commit v1 on v0

--- a/solution.py
+++ b/solution.py
@@ -4,6 +4,12 @@
 from jax.sharding import PartitionSpec as P
 
 OPPOSE = (1, 0, 3, 2, 5, 4)
+
+
+def gather_and_add(block, mesh_axis):
+    pieces = lax.all_gather(block, mesh_axis, axis=0, tiled=False)
+    acc = pieces.sum(axis=0)
+    return acc
 
 
 def extended(cells, sides, width):
@@ -188,7 +194,7 @@
         total_one = total_one + ratios_one[index]
     grad_potential = grad_potential + whole_one * total_one
     grad_unary = potential * grad_potential
-    summed = lax.psum(weights_two + weights_one, ("gx", "gy", "gz"))
+    summed = gather_and_add(weights_two + weights_one, ("gx", "gy", "gz"))
     grad_compat = weights * summed
     return (grad_unary, grad_compat)
 

time: 414 us -> 1020 us (2.46)
  waiting for transfers between devices: 256 us -> 830 us
  other arithmetic: 48.6 us -> 75.9 us
    all_gather x0 -> x1, waiting for transfers between devices: none -> 830 us  [gather_and_add(): pieces = lax.all_gather(block, mesh_axis, axis=0, tiled=False)]
    psum x1 -> x0, waiting for transfers between devices: 256 us -> none  [body(): summed = lax.psum(weights_two + weights_one, ('gx', 'gy', 'gz'))]
    reduce_sum x0 -> x1, other arithmetic: none -> 30.8 us  [gather_and_add(): acc = pieces.sum(axis=0)]
  transfers between devices with their start and end apart: 19 -> 19, of which waited for: 3 -> 3; matrix products, arithmetic and copies ran while one was open for 7% -> 3% of each run, Pallas kernels for 0% -> 0%
where the time goes in v1:
time: 1020 us
  waiting for transfers between devices  830 us (81%)
  other arithmetic  75.9 us (7%)
  starting transfers between devices  53 us (5%)
  matrix products  31.7 us (3%)
  between operations  15.2 us (1%)
    all_gather x1, waiting for transfers between devices, gather_and_add(): pieces = lax.all_gather(block, mesh_axis, axis=0, tiled=False)  830 us
    ppermute x9, starting transfers between devices, extended(): lax.ppermute(tail, axis, [(i, (i + 1) % count) for i in range(ends)])  34.2 us
    reduce_sum x1, other arithmetic, gather_and_add(): acc = pieces.sum(axis=0)  30.8 us
  transfers between devices with their start and end apart: 19, of which 3 were waited for; matrix products, arithmetic and copies ran while one was open for 3% of the time, Pallas kernels for 0%

profile of v1, /device:TPU:1, one launch (start us, length us, event | category | flops | bytes accessed | tf_op | source)
XLA Modules:
  0.0 1015.7 jit_solution(13061591113713065218)
XLA Ops:
  7.2 1.1 fusion.68
  8.3 4.7 bitcast_dynamic-update-slice_fusion.5
  13.0 0.2 bitcast_dynamic-update-slice_fusion.4
  13.2 0.2 bitcast_dynamic-update-slice_fusion.3
  13.5 1.4 copy-done
  15.1 0.2 bitcast_dynamic-update-slice_fusion.9
  15.6 0.2 bitcast_dynamic-update-slice_fusion.7
  15.8 0.4 bitcast_dynamic-update-slice_fusion.2
  16.2 1.9 fusion.77
  18.1 2.0 fusion.13
  20.1 0.7 copy-done.3
  21.0 0.7 slice.299
  21.7 1.3 collective-permute-start.5
  23.0 0.6 slice.295
  23.6 4.9 collective-permute-start.4
  28.6 0.6 slice.293
  29.2 1.3 collective-permute-start.3
  30.5 0.6 slice.289
  31.1 4.3 collective-permute-start.2
  35.4 0.7 slice_bitcast_fusion.19
  36.1 5.6 collective-permute-start.1
  41.7 0.9 slice_bitcast_fusion.17
  42.6 0.2 bitcast_dynamic-update-slice_fusion.1
  42.8 0.2 bitcast_dynamic-update-slice_fusion
  43.1 4.4 fusion.78
  47.5 0.6 broadcast_divide_fusion.1
  48.1 1.0 slice.298
  49.1 1.1 slice.290
  50.2 2.2 collective-permute-start
  52.5 0.8 broadcast_select_fusion.4
  53.3 0.9 broadcast_select_fusion.2
  54.2 0.9 broadcast_select_fusion
  55.1 2.0 fusion.72
  57.2 11.9 %fusion.37 = (bf16[4,8,64,128]{3,2,1,0:T(8,128)(2,1)S(1)}, f32[4,8,64,128]{3,2,1,0:T(8,128)S(1)}, f32[4,8,64,128]{3,2,1,0:T(8,128)}) fusion(bf16[4,8,1,128]{3,2,1,0:T(2,128)(2,1)S(1)} %broadcast_select_fusion.4, bf16[4,8,63,128]{3,2,1,0:T(8,128)(2,1)S(1)} %copy-done.19, f32[4,8,64,128]{3,2,1,0:T(8,128)S(1)} %get-tuple-element.13, ...), kind=kOutput, calls=%fused_computation.75 | output fusion | flops 4196479 | bytes 5775360 | tf_op jit(solution)/shard_map/sub | solution.py:122
  69.1 0.8 fusion.36
  70.0 2.5 collective-permute-start.6
  72.5 3.2 collective-permute-start.7
  76.1 1.4 collective-permute-start.8
  77.6 4.0 collective-permute-start.9
  81.6 1.3 collective-permute-start.10
  82.9 4.0 collective-permute-start.11
  87.3 0.4 collective-permute-done.11
  87.8 0.2 fusion.60
  88.0 3.8 fusion.1
  91.8 5.5 fusion.79
  97.4 1.1 multiply_convert_fusion
  98.5 0.5 multiply_convert_fusion.1
  98.9 1.0 multiply_convert_fusion.5
  99.9 2.9 collective-permute-start.12
  102.8 1.2 multiply_convert_fusion.2
  104.0 3.4 collective-permute-start.13
  107.5 5.7 fusion.17
  113.5 1.3 collective-permute-start.14
  114.8 4.0 collective-permute-start.15
  118.8 1.3 collective-permute-start.16
  120.1 4.2 collective-permute-start.17
  125.0 0.2 fusion.66
  125.3 3.8 fusion.4
  129.1 6.3 fusion.27
  135.5 8.0 fusion.80
  143.5 4.0 fusion.46
  147.5 829.7 %all-gather.3.cloned.1.call-done = f32[1536,128,128]{2,1,0:T(8,128)} async-done(((f32[6,128,128]{2,1,0:T(8,128)}), f32[1536,128,128]{2,1,0:T(8,128)}) %all-gather.3.cloned.1.call-update) | async-done | bytes 100663312 | tf_op jit(solution)/shard_map/all_gather | solution.py:10
  977.3 30.8 %reduce_sum.69 = f32[6,128,128]{2,1,0:T(8,128)S(1)} reduce(f32[256,6,128,128]{3,2,1,0:T(8,128)} %bitcast.75, f32[]{:T(128)} %constant.7.clone.1), dimensions={0}, to_apply=%region_6.7 | reduce | flops 25067520 | bytes 101056512 | tf_op jit(solution)/shard_map/reduce_sum | solution.py:11
  1008.0 0.8 exponential_multiply_fusion
  (122 shorter events, 2.6 us)
Async XLA Ops:
  7.2 970.1 %all-gather.3.cloned.1.call-start = ((), (), s32[]{:S(2)}) async-start(), calls=%async_computation | async-start | bytes 101056512 | tf_op jit(solution)/shard_map/all_gather | solution.py:10
  8.3 4.7 copy-start.4
  13.0 1.9 copy-start
  16.2 1.9 copy-start.11
  18.1 2.7 copy-start.3
  21.0 21.8 %copy-start.21 = (bf16[4,8,64,128]{3,2,1,0:T(8,128)(2,1)}, bf16[4,8,64,128]{3,2,1,0:T(8,128)(2,1)S(1)}, u32[]{:S(2)}) copy-start(bf16[4,8,64,128]{3,2,1,0:T(8,128)(2,1)S(1)} %get-tuple-element.23) | copy-start | bytes 1572868
  21.7 28.5 %collective-permute-start.5 = (bf16[4,8,1,128]{3,2,1,0:T(2,128)(2,1)}, bf16[4,8,1,128]{3,2,1,0:T(2,128)(2,1)}, u32[]{:S(2)}, u32[]{:S(2)}) collective-permute-start(bf16[4,8,1,128]{3,2,1,0:T(2,128)(2,1)} %slice.299), channel_id=1, source_target_pairs={{1,0},{3,2},{5,4},{7,6},{9,8},{11,10},{13,12},{15,14},{17,16},{19,... | collective-permute-start | bytes 24584 | tf_op jit(solution)/shard_map/ppermute | solution.py:25
  23.6 29.6 %collective-permute-start.4 = (bf16[4,8,1,128]{3,2,1,0:T(2,128)(2,1)}, bf16[4,8,1,128]{3,2,1,0:T(2,128)(2,1)S(1)}, u32[]{:S(2)}, u32[]{:S(2)}) collective-permute-start(bf16[4,8,1,128]{3,2,1,0:T(2,128)(2,1)} %slice.295), channel_id=1, source_target_pairs={{0,1},{2,3},{4,5},{6,7},{8,9},{10,11},{12,13},{14,15},{16,17},{18,... | collective-permute-start | bytes 24584 | tf_op jit(solution)/shard_map/ppermute | solution.py:23
  29.2 24.1 %collective-permute-start.3 = (bf16[4,1,64,128]{3,2,1,0:T(8,128)(2,1)}, bf16[4,1,64,128]{3,2,1,0:T(8,128)(2,1)}, u32[]{:S(2)}, u32[]{:S(2)}) collective-permute-start(bf16[4,1,64,128]{3,2,1,0:T(8,128)(2,1)} %slice.293), channel_id=1, source_target_pairs={{2,0},{4,2},{6,4},{3,1},{5,3},{7,5},{10,8},{12,10},{14,12},{11,9},... | collective-permute-start | bytes 196616 | tf_op jit(solution)/shard_map/ppermute | solution.py:25
  31.1 23.0 %collective-permute-start.2 = (bf16[4,1,64,128]{3,2,1,0:T(8,128)(2,1)}, bf16[4,1,64,128]{3,2,1,0:T(8,128)(2,1)S(1)}, u32[]{:S(2)}, u32[]{:S(2)}) collective-permute-start(bf16[4,1,64,128]{3,2,1,0:T(8,128)(2,1)} %slice.289), channel_id=1, source_target_pairs={{0,2},{2,4},{4,6},{1,3},{3,5},{5,7},{8,10},{10,12},{12,14},{9,11},... | collective-permute-start | bytes 196616 | tf_op jit(solution)/shard_map/ppermute | solution.py:23
  36.1 18.1 %collective-permute-start.1 = (bf16[1,8,64,128]{3,2,1,0:T(8,128)(2,1)}, bf16[1,8,64,128]{3,2,1,0:T(8,128)(2,1)}, u32[]{:S(2)}, u32[]{:S(2)}) collective-permute-start(bf16[1,8,64,128]{3,2,1,0:T(8,128)(2,1)} %get-tuple-element.20), channel_id=1, source_target_pairs={{8,0},{16,8},{24,16},{32,24},{40,32},{48,40},{56,48},{64,56},{72,6... | collective-permute-start | bytes 393224 | tf_op jit(solution)/shard_map/ppermute | solution.py:25
  43.1 4.4 copy-start.13
  47.5 7.7 copy-start.9
  50.2 7.0 copy-start.19
  50.2 7.0 copy-start.25
  50.2 4.9 collective-permute-start
  57.2 11.9 %copy-start.15 = (f32[4,8,64,128]{3,2,1,0:T(8,128)}, f32[4,8,64,128]{3,2,1,0:T(8,128)S(1)}, u32[]{:S(2)}) copy-start(f32[4,8,64,128]{3,2,1,0:T(8,128)S(1)} %get-tuple-element.13) | copy-start | bytes 3145732
  57.2 11.9 %copy-start.17 = (bf16[3,8,64,128]{3,2,1,0:T(8,128)(2,1)S(1)}, bf16[3,8,64,128]{3,2,1,0:T(8,128)(2,1)}, u32[]{:S(2)}) copy-start(bf16[3,8,64,128]{3,2,1,0:T(8,128)(2,1)} %get-tuple-element.21) | copy-start | bytes 1179652
  57.2 11.9 %copy-start.18 = (bf16[3,8,64,128]{3,2,1,0:T(8,128)(2,1)S(1)}, bf16[3,8,64,128]{3,2,1,0:T(8,128)(2,1)}, u32[]{:S(2)}) copy-start(bf16[3,8,64,128]{3,2,1,0:T(8,128)(2,1)} %get-tuple-element.22) | copy-start | bytes 1179652
  69.1 18.9 %slice-start = ((s8[6291456]{0:T(1024)(128)(4,1)}), s8[4194304]{0:T(1024)(128)(4,1)S(1)}, s32[]{:S(2)}) async-start(s8[6291456]{0:T(1024)(128)(4,1)} %bitcast.354), calls=%async_computation.1 | async-start | bytes 8388608
  70.0 12.9 %collective-permute-start.6 = (bf16[1,8,64,128]{3,2,1,0:T(8,128)(2,1)S(1)}, bf16[1,8,64,128]{3,2,1,0:T(8,128)(2,1)S(1)}, u32[]{:S(2)}, u32[]{:S(2)}) collective-permute-start(bf16[1,8,64,128]{3,2,1,0:T(8,128)(2,1)S(1)} %slice.301), channel_id=1, source_target_pairs={{8,0},{16,8},{24,16},{32,24},{40,32},{48,40},{56,48},{64,56},{72,6... | collective-permute-start | bytes 393224 | tf_op jit(solution)/shard_map/ppermute | solution.py:25
  72.5 14.4 %collective-permute-start.7 = (bf16[1,8,64,128]{3,2,1,0:T(8,128)(2,1)S(1)}, bf16[1,8,64,128]{3,2,1,0:T(8,128)(2,1)S(1)}, u32[]{:S(2)}, u32[]{:S(2)}) collective-permute-start(bf16[1,8,64,128]{3,2,1,0:T(8,128)(2,1)S(1)} %slice.302), channel_id=1, source_target_pairs={{0,8},{8,16},{16,24},{24,32},{32,40},{40,48},{48,56},{56,64},{64,7... | collective-permute-start | bytes 393224 | tf_op jit(solution)/shard_map/ppermute | solution.py:23
  75.7 53.4 %copy-start.24 = (f32[6,4,8,64]{3,2,1,0:T(8,128)}, f32[6,4,8,64]{3,2,1,0:T(8,128)S(1)}, u32[]{:S(2)}) copy-start(f32[6,4,8,64]{3,2,1,0:T(8,128)S(1)} %broadcast_divide_fusion) | copy-start | bytes 147460
  75.8 12.2 %slice-start.1 = ((s8[6291456]{0:T(1024)(128)(4,1)}), s8[2097152]{0:T(1024)(128)(4,1)S(1)}, s32[]{:S(2)}) async-start(s8[6291456]{0:T(1024)(128)(4,1)} %bitcast.354), calls=%async_computation.2 | async-start | bytes 4194304
  76.1 10.9 %collective-permute-start.8 = (bf16[4,1,64,128]{3,2,1,0:T(8,128)(2,1)S(1)}, bf16[4,1,64,128]{3,2,1,0:T(8,128)(2,1)S(1)}, u32[]{:S(2)}, u32[]{:S(2)}) collective-permute-start(bf16[4,1,64,128]{3,2,1,0:T(8,128)(2,1)S(1)} %slice.305), channel_id=1, source_target_pairs={{2,0},{4,2},{6,4},{3,1},{5,3},{7,5},{10,8},{12,10},{14,12},{11,9},... | collective-permute-start | bytes 196616 | tf_op jit(solution)/shard_map/ppermute | solution.py:25
  77.6 9.6 collective-permute-start.9
  81.6 5.6 collective-permute-start.10
  82.9 4.8 collective-permute-start.11
  88.0 3.8 copy-start.23
  91.8 5.5 copy-start.1
  98.5 1.4 copy-start.7
  99.9 13.3 %copy-start.20 = (bf16[4,8,64,128]{3,2,1,0:T(8,128)(2,1)}, bf16[4,8,64,128]{3,2,1,0:T(8,128)(2,1)S(1)}, u32[]{:S(2)}) copy-start(bf16[4,8,64,128]{3,2,1,0:T(8,128)(2,1)S(1)} %multiply_convert_fusion.5) | copy-start | bytes 1572868
  99.9 20.2 %collective-permute-start.12 = (bf16[1,8,64,128]{3,2,1,0:T(8,128)(2,1)S(1)}, bf16[1,8,64,128]{3,2,1,0:T(8,128)(2,1)S(1)}, u32[]{:S(2)}, u32[]{:S(2)}) collective-permute-start(bf16[1,8,64,128]{3,2,1,0:T(8,128)(2,1)S(1)} %slice.319), channel_id=1, source_target_pairs={{8,0},{16,8},{24,16},{32,24},{40,32},{48,40},{56,48},{64,56},{72,6... | collective-permute-start | bytes 393224 | tf_op jit(solution)/shard_map/ppermute | solution.py:25
  102.8 4.7 copy-start.12
  102.8 22.4 %slice-start.2 = ((s8[6291456]{0:T(1024)(128)(4,1)}), s8[2097152]{0:T(1024)(128)(4,1)S(1)}, s32[]{:S(2)}) async-start(s8[6291456]{0:T(1024)(128)(4,1)} %bitcast.356), calls=%async_computation.3 | async-start | bytes 4194304
  104.0 21.2 %slice-start.3 = ((s8[6291456]{0:T(1024)(128)(4,1)}), s8[4194304]{0:T(1024)(128)(4,1)S(1)}, s32[]{:S(2)}) async-start(s8[6291456]{0:T(1024)(128)(4,1)} %bitcast.356), calls=%async_computation.4 | async-start | bytes 8388608
  104.0 20.4 %collective-permute-start.13 = (bf16[1,8,64,128]{3,2,1,0:T(8,128)(2,1)S(1)}, bf16[1,8,64,128]{3,2,1,0:T(8,128)(2,1)S(1)}, u32[]{:S(2)}, u32[]{:S(2)}) collective-permute-start(bf16[1,8,64,128]{3,2,1,0:T(8,128)(2,1)S(1)} %slice.320), channel_id=1, source_target_pairs={{0,8},{8,16},{16,24},{24,32},{32,40},{40,48},{48,56},{56,64},{64,7... | collective-permute-start | bytes 393224 | tf_op jit(solution)/shard_map/ppermute | solution.py:23
  113.2 11.2 %slice-start.4 = ((bf16[4,8,64,128]{3,2,1,0:T(8,128)(2,1)}), bf16[3,8,64,128]{3,2,1,0:T(8,128)(2,1)S(1)}, s32[]{:S(2)}) async-start(bf16[4,8,64,128]{3,2,1,0:T(8,128)(2,1)} %copy-done.20), calls=%async_computation.5 | async-start | bytes 786432 | tf_op jit(solution)/shard_map/slice | solution.py:105
  113.5 11.0 %collective-permute-start.14 = (bf16[4,1,64,128]{3,2,1,0:T(8,128)(2,1)S(1)}, bf16[4,1,64,128]{3,2,1,0:T(8,128)(2,1)S(1)}, u32[]{:S(2)}, u32[]{:S(2)}) collective-permute-start(bf16[4,1,64,128]{3,2,1,0:T(8,128)(2,1)S(1)} %slice.323), channel_id=1, source_target_pairs={{2,0},{4,2},{6,4},{3,1},{5,3},{7,5},{10,8},{12,10},{14,12},{11,9},... | collective-permute-start | bytes 196616 | tf_op jit(solution)/shard_map/ppermute | solution.py:25
  114.8 9.8 collective-permute-start.15
  118.8 5.9 collective-permute-start.16
  120.1 4.8 collective-permute-start.17
  125.2 3.9 copy-start.6
  125.3 3.9 copy-start.14
  135.4 8.1 copy-start.2
  135.4 8.1 copy-start.5
  135.4 8.1 copy-start.8
  135.5 8.1 copy-start.10
  135.5 8.1 copy-start.16
  977.3 30.8 %copy-start.22 = (f32[6,128,128]{2,1,0:T(8,128)S(1)}, f32[6,128,128]{2,1,0:T(8,128)}, u32[]{:S(2)}) copy-start(f32[6,128,128]{2,1,0:T(8,128)} %param.6) | copy-start | bytes 1179652
Sparse Core Ops, SparseCore 0:
  135.5 841.6 all-gather.2
